TPU v7x, 32 devices: a whole 2x2x4 slice. The times are simulated.
32 devices in a mesh: groups: 2 (over x), dp: 16 (over z, y, core).
Axes of the slice: x: 2, y: 2, z: 4, core: 2. Of those that a mesh axis runs over, the one named last changes fastest.
Arguments:
- frames: bfloat16 [128, 256, 1536], P(('groups', 'dp')), parts along dimension 0, may hold values from -6 to 6
- cotangent: bfloat16 [128, 256, 1536], P(('groups', 'dp')), parts along dimension 0, may hold values from -6 to 6
- gain: float32 [1536], replicated, may hold values from 0.25 to 1.75
- down_weight: bfloat16 [320, 1536, 256], P('groups', 'dp'), parts along dimension 0, may hold values from -0.15625 to 0.15625
- up_weight: bfloat16 [320, 1536, 256], P('groups', 'dp'), parts along dimension 0, may hold values from -0.375 to 0.375
- slot_lang: int32 [32, 2], P('groups'), parts along dimension 0, may hold values from 0 to 159
- utt_slot: int32 [128], P('groups'), parts along dimension 0, may hold values from 0 to 1
- lengths: int32 [128], P('groups'), parts along dimension 0, may hold values from 64 to 256
Outputs:
- frame_grads: bfloat16 [128, 256, 1536], P(('groups', 'dp')), parts along dimension 0
- down_grads: bfloat16 [320, 1536, 256], P('groups', 'dp'), parts along dimension 0
- up_grads: bfloat16 [320, 1536, 256], P('groups', 'dp'), parts along dimension 0
There are 2 independent parts, one for each index of `groups`. A program takes and returns all parts, laid end to end along the dimension named above; an argument that names none is the same for every part. Nothing has to cross between parts.
All inputs are finite; a program needn't handle non-finite values.
Results may differ from a plain program's by a relative error of at most 0.0061.
Values may be sent and summed in bfloat16 or wider, within the bound.
No kernel may reach another device: no remote copies, remote signals or barrier semaphores. Data moves between devices by JAX's collectives and lax.ppermute only.
A program may use at most 128 MiB of HBM per device.

v0:
```python
import jax
import jax.numpy as jnp
from jax import lax
from jax.sharding import PartitionSpec as P


def local_pass(frames, cotangent, gain, w_down, w_up, live_mask, slot_select):
    values = frames.astype(jnp.float32)
    centre_mean = jnp.mean(values, axis=2, keepdims=True)
    mean_removed = values - centre_mean
    variance = jnp.mean(mean_removed * mean_removed, axis=2, keepdims=True)
    reciprocal_deviation = lax.rsqrt(variance + 1e-06)
    standardized_input = mean_removed * reciprocal_deviation
    layer_normed = (standardized_input * gain).astype(jnp.bfloat16)
    pre_act = jnp.einsum("ufd,udr->ufr", layer_normed, w_down, preferred_element_type=jnp.float32)
    sigmoid_pre = jax.nn.sigmoid(pre_act)
    hidden = (pre_act * sigmoid_pre).astype(jnp.bfloat16)
    masked_up = jnp.where(live_mask, cotangent, jnp.zeros_like(cotangent))
    hidden_slots = hidden[None] * slot_select[:, :, None, None]
    grad_up = jnp.einsum(
        "ufd,sufr->sdr", masked_up, hidden_slots, preferred_element_type=jnp.float32
    )
    d_hidden = jnp.einsum("ufd,udr->ufr", masked_up, w_up, preferred_element_type=jnp.float32)
    d_pre = (d_hidden * sigmoid_pre * (1.0 + pre_act * (1.0 - sigmoid_pre))).astype(jnp.bfloat16)
    d_pre_slots = d_pre[None] * slot_select[:, :, None, None]
    grad_down = jnp.einsum(
        "ufd,sufr->sdr", layer_normed, d_pre_slots, preferred_element_type=jnp.float32
    )
    d_normed = jnp.einsum("ufr,udr->ufd", d_pre, w_down, preferred_element_type=jnp.float32)
    scaled_rows = d_normed * gain
    inner_gradient = (
        scaled_rows
        - jnp.mean(scaled_rows, axis=2, keepdims=True)
        - standardized_input * jnp.mean(scaled_rows * standardized_input, axis=2, keepdims=True)
    ) * reciprocal_deviation
    d_frames = (cotangent.astype(jnp.float32) + inner_gradient).astype(jnp.bfloat16)
    return (d_frames, grad_down, grad_up)


def on_device(frames, cotangent, gain, down_weight, up_weight, slot_lang, utt_slot, lengths):
    devices = lax.axis_size("dp")
    self_index = lax.axis_index("dp")
    per_device = frames.shape[0]
    slots = slot_lang.shape[1]
    lang_count, row_count, bottleneck = down_weight.shape
    owners = jnp.arange(utt_slot.shape[0], dtype=jnp.int32) // per_device
    utt_lang = slot_lang[owners, utt_slot]
    own_lengths = lax.dynamic_slice_in_dim(lengths, self_index * per_device, per_device)
    own_slot = lax.dynamic_slice_in_dim(utt_slot, self_index * per_device, per_device)
    live_mask = (jnp.arange(frames.shape[1], dtype=jnp.int32)[None, :] < own_lengths[:, None])[
        :, :, None
    ]
    lang_ids = jnp.arange(lang_count, dtype=jnp.int32)
    counts = jnp.sum(jnp.where(utt_lang[None, :] == lang_ids[:, None], lengths[None, :], 0), axis=1)
    scaling = lax.rsqrt(jnp.maximum(counts, 1).astype(jnp.float32))
    member_langs = slot_lang.T.reshape(-1)
    send_down = jnp.take(down_weight, member_langs, axis=0).reshape(
        slots, devices, row_count, bottleneck
    )
    send_up = jnp.take(up_weight, member_langs, axis=0).reshape(
        slots, devices, row_count, bottleneck
    )
    got_down = lax.all_to_all(send_down, "dp", split_axis=1, concat_axis=1, tiled=True)
    got_up = lax.all_to_all(send_up, "dp", split_axis=1, concat_axis=1, tiled=True)
    got_down = got_down.reshape(slots, devices * row_count, bottleneck)
    got_up = got_up.reshape(slots, devices * row_count, bottleneck)
    w_down = jnp.take(got_down, own_slot, axis=0)
    w_up = jnp.take(got_up, own_slot, axis=0)
    slot_select = (jnp.arange(slots, dtype=jnp.int32)[:, None] == own_slot[None, :]).astype(
        jnp.bfloat16
    )
    d_frames, grad_down, grad_up = local_pass(
        frames, cotangent, gain, w_down, w_up, live_mask, slot_select
    )
    own_scale = jnp.take(scaling, lax.dynamic_index_in_dim(slot_lang, self_index, 0, False))
    own_scale = own_scale[:, None, None]

    def exchange_back(grad):
        scaled = (grad * own_scale).astype(jnp.bfloat16)
        scaled = scaled.reshape(slots, devices, row_count, bottleneck)
        back = lax.all_to_all(scaled, "dp", split_axis=1, concat_axis=1, tiled=True)
        return back.reshape(slots * devices, row_count, bottleneck)

    back_down = exchange_back(grad_down)
    back_up = exchange_back(grad_up)
    lang_table = (lang_ids[:, None] == member_langs[None, :]).astype(jnp.bfloat16)
    down_grads = jnp.einsum(
        "lm,mkr->lkr", lang_table, back_down, preferred_element_type=jnp.float32
    ).astype(jnp.bfloat16)
    up_grads = jnp.einsum(
        "lm,mkr->lkr", lang_table, back_up, preferred_element_type=jnp.float32
    ).astype(jnp.bfloat16)
    return (d_frames, down_grads, up_grads)


def solution(mesh):
    placed = (
        P(("groups", "dp"), None, None),
        P(("groups", "dp"), None, None),
        P(),
        P("groups", "dp", None),
        P("groups", "dp", None),
        P("groups", None),
        P("groups"),
        P("groups"),
    )
    return jax.shard_map(
        on_device,
        mesh=mesh,
        in_specs=placed,
        out_specs=(
            P(("groups", "dp"), None, None),
            P("groups", "dp", None),
            P("groups", "dp", None),
        ),
        check_vma=False,
    )
```

profile of v0, /device:TPU:13, one launch (start us, length us, event | category | flops | bytes accessed | tf_op | source)
XLA Modules:
  0.0 215.7 jit_solution(16785040773158458793)
XLA Ops:
  1.4 3.9 %gather_fusion.4 = bf16[32,96,256]{2,1,0:T(8,128)(2,1)S(1)} fusion(bf16[160,96,256]{2,1,0:T(8,128)(2,1)} %param.15, s32[1024]{0:T(1024)S(1)} %pad_clamp_fusion.2), kind=kCustom, calls=%fused_computation.2.clone | custom fusion | bytes 3145856 | tf_op jit(solution)/shard_map/jit(_take)/gather | solution.py:57
  5.3 3.9 %gather_fusion.2 = bf16[32,96,256]{2,1,0:T(8,128)(2,1)S(1)} fusion(bf16[160,96,256]{2,1,0:T(8,128)(2,1)} %param.16, s32[1024]{0:T(1024)S(1)} %pad_clamp_fusion.2), kind=kCustom, calls=%fused_computation.clone | custom fusion | bytes 3145856 | tf_op jit(solution)/shard_map/jit(_take)/gather | solution.py:60
  12.0 6.6 %all-to-all-start.1 = ((bf16[2,16,96,256]{3,2,0,1:T(8,128)(2,1)}), bf16[2,16,96,256]{3,2,0,1:T(8,128)(2,1)}, u32[]{:S(2)}, u32[]{:S(2)}) async-start(bf16[2,16,96,256]{3,2,0,1:T(8,128)(2,1)} %copy.51), calls=%async_computation.1 | async-start | bytes 3145728 | tf_op jit(solution)/shard_map/all_to_all | solution.py:63
  18.6 2.8 %copy.49 = bf16[2,16,96,256]{3,2,0,1:T(8,128)(2,1)} copy(bf16[2,16,96,256]{3,2,1,0:T(8,128)(2,1)} %bitcast.69) | data formatting | bytes 3145728 | tf_op jit(solution)/shard_map/reshape | solution.py:60
  21.4 33.4 %all-to-all-done.1 = bf16[2,16,96,256]{3,2,0,1:T(8,128)(2,1)} async-done(((bf16[2,16,96,256]{3,2,0,1:T(8,128)(2,1)}), bf16[2,16,96,256]{3,2,0,1:T(8,128)(2,1)}, u32[]{:S(2)}, u32[]{:S(2)}) %all-to-all-start.1) | async-done | bytes 1572896 | tf_op jit(solution)/shard_map/all_to_all | solution.py:63
  54.8 4.9 %all-to-all-start = ((bf16[2,16,96,256]{3,2,0,1:T(8,128)(2,1)}), bf16[2,16,96,256]{3,2,0,1:T(8,128)(2,1)}, u32[]{:S(2)}, u32[]{:S(2)}) async-start(bf16[2,16,96,256]{3,2,0,1:T(8,128)(2,1)} %copy.49), calls=%async_computation | async-start | bytes 3145728 | tf_op jit(solution)/shard_map/all_to_all | solution.py:64
  63.3 2.7 %copy.52 = bf16[2,16,96,256]{3,2,1,0:T(8,128)(2,1)} copy(bf16[2,16,96,256]{3,2,0,1:T(8,128)(2,1)} %all-to-all-done.1) | data formatting | bytes 3145728 | tf_op jit(solution)/shard_map/all_to_all | solution.py:63
  66.0 3.8 %gather_fusion.5 = bf16[4,1536,256]{2,1,0:T(8,128)(2,1)} fusion(bf16[2,1536,256]{2,1,0:T(8,128)(2,1)} %bitcast.64, s32[1024]{0:T(1024)S(1)} %pad_clamp_fusion.1), kind=kCustom, calls=%fused_computation.3.clone | custom fusion | bytes 6291472 | tf_op jit(solution)/shard_map/jit(_take)/gather | solution.py:67
  69.8 26.2 %all-to-all-done = bf16[2,16,96,256]{3,2,0,1:T(8,128)(2,1)} async-done(((bf16[2,16,96,256]{3,2,0,1:T(8,128)(2,1)}), bf16[2,16,96,256]{3,2,0,1:T(8,128)(2,1)}, u32[]{:S(2)}, u32[]{:S(2)}) %all-to-all-start) | async-done | bytes 1572896 | tf_op jit(solution)/shard_map/all_to_all | solution.py:64
  96.0 2.7 %copy.50 = bf16[2,16,96,256]{3,2,1,0:T(8,128)(2,1)} copy(bf16[2,16,96,256]{3,2,0,1:T(8,128)(2,1)} %all-to-all-done) | data formatting | bytes 3145728 | tf_op jit(solution)/shard_map/all_to_all | solution.py:64
  98.7 3.8 %gather_fusion.3 = bf16[4,1536,256]{2,1,0:T(8,128)(2,1)} fusion(bf16[2,1536,256]{2,1,0:T(8,128)(2,1)} %bitcast.63, s32[1024]{0:T(1024)S(1)} %pad_clamp_fusion.1), kind=kCustom, calls=%fused_computation.1.clone | custom fusion | bytes 6291472 | tf_op jit(solution)/shard_map/jit(_take)/gather | solution.py:68
  102.5 4.4 %multiply_convert_fusion = (bf16[4,256,256]{2,1,0:T(8,128)(2,1)}, f32[4,256,256]{2,1,0:T(8,128)S(1)}) fusion(bf16[4,1536,256]{2,1,0:T(8,128)(2,1)} %gather_fusion.5, pred[4]{0:T(512)(128)(4,1)S(1)} %get-tuple-element.22, bf16[4,256,1536]{2,1,0:T(8,128)(2,1)S(1)} %copy-done.1, f32[1536]{0:T(1024)S(1)} %copy-done.5, f32[4,256]{1,0:T(4,128)S(1)} %add_rsqrt_fusion, ...), kind=kOutput, calls=%fused_computation.49 | convolution fusion | flops 816054272 | bytes 7878660 | tf_op jit(solution)/shard_map/ufd,udr->ufr/dot_general | solution.py:15
  111.1 4.2 %fusion.28 = bf16[2,1536,256]{1,2,0:T(8,128)(2,1)} fusion(bf16[4,256,1536]{2,1,0:T(8,128)(2,1)S(1)} %copy-done.1, f32[1536]{0:T(1024)S(1)} %copy-done.5, f32[4,256]{1,0:T(4,128)S(1)} %add_rsqrt_fusion, f32[4,256]{1,0:T(4,128)S(1)} %broadcast_multiply_fusion.2, f32[2]{0:T(128)S(1)} %and_select_fusion.1, bf16[2,4]{1,0:T(2,128)(2,1)S(1)} %compare_convert_fusion, ...), kind=kOutput, calls=%fused_computation.37 | convolution fusion | flops 1620574208 | bytes 5257240 | tf_op jit(solution)/shard_map/ufd,sufr->sdr/dot_general | solution.py:26
  117.9 2.7 %copy.55 = bf16[2,16,96,256]{3,2,0,1:T(8,128)(2,1)} copy(bf16[2,16,96,256]{3,2,1,0:T(8,128)(2,1)} %bitcast.66) | data formatting | bytes 3145728 | tf_op jit(solution)/shard_map/reshape | solution.py:80
  120.6 4.9 %all-to-all-start.2 = ((bf16[2,16,96,256]{3,2,0,1:T(8,128)(2,1)}), bf16[2,16,96,256]{3,2,0,1:T(8,128)(2,1)}, u32[]{:S(2)}, u32[]{:S(2)}) async-start(bf16[2,16,96,256]{3,2,0,1:T(8,128)(2,1)} %copy.55), calls=%async_computation.2 | async-start | bytes 3145728 | tf_op jit(solution)/shard_map/all_to_all | solution.py:81
  127.6 5.1 %fusion.25 = bf16[2,1536,256]{1,2,0:T(8,128)(2,1)} fusion(bf16[4,256,1536]{2,1,0:T(8,128)(2,1)} %param.13, pred[4,256]{1,0:T(4,128)(4,1)S(1)} %iota_compare_fusion.2, f32[2]{0:T(128)S(1)} %and_select_fusion.1, bf16[4,256,256]{1,2,0:T(8,128)(2,1)} %copy.57, bf16[2,4]{1,0:T(2,128)(2,1)S(1)} %compare_convert_fusion), kind=kOutput, calls=%fused_computation.36 | convolution fusion | flops 1614282752 | bytes 5243928 | tf_op jit(solution)/shard_map/ufd,sufr->sdr/dot_general | solution.py:20
  135.2 2.7 %copy.59 = bf16[2,16,96,256]{3,2,0,1:T(8,128)(2,1)} copy(bf16[2,16,96,256]{3,2,1,0:T(8,128)(2,1)} %bitcast.67) | data formatting | bytes 3145728 | tf_op jit(solution)/shard_map/reshape | solution.py:80
  137.9 23.9 %all-to-all-done.2 = bf16[2,16,96,256]{3,2,0,1:T(8,128)(2,1)} async-done(((bf16[2,16,96,256]{3,2,0,1:T(8,128)(2,1)}), bf16[2,16,96,256]{3,2,0,1:T(8,128)(2,1)}, u32[]{:S(2)}, u32[]{:S(2)}) %all-to-all-start.2) | async-done | bytes 1572896 | tf_op jit(solution)/shard_map/all_to_all | solution.py:81
  161.8 4.9 %all-to-all-start.3 = ((bf16[2,16,96,256]{3,2,0,1:T(8,128)(2,1)}), bf16[2,16,96,256]{3,2,0,1:T(8,128)(2,1)}, u32[]{:S(2)}, u32[]{:S(2)}) async-start(bf16[2,16,96,256]{3,2,0,1:T(8,128)(2,1)} %copy.59), calls=%async_computation.3 | async-start | bytes 3145728 | tf_op jit(solution)/shard_map/all_to_all | solution.py:81
  166.7 4.6 %multiply_reduce_fusion = (f32[4,256]{1,0:T(4,128)S(1)}, f32[4,256]{1,0:T(4,128)S(1)}, f32[4,256,1536]{2,1,0:T(8,128)S(1)}) fusion(f32[1536]{0:T(1024)S(1)} %copy-done.5, f32[4,256]{1,0:T(4,128)S(1)} %add_rsqrt_fusion, f32[4,256]{1,0:T(4,128)S(1)} %broadcast_multiply_fusion.2, bf16[4,256,1536]{2,1,0:T(8,128)(2,1)S(1)} %copy-done.1, ...), kind=kOutput, calls=%fused_computation.22 | convolution fusion | flops 817887232 | bytes 13129732 | tf_op jit(solution)/shard_map/ufr,udr->ufd/dot_general | solution.py:29
  171.4 4.0 %fusion.10 = bf16[4,256,1536]{2,1,0:T(8,128)(2,1)} fusion(bf16[4,256,1536]{2,1,0:T(8,128)(2,1)S(1)} %copy-done.1, bf16[4,256,1536]{2,1,0:T(8,128)(2,1)S(1)} %copy-done.4, f32[4,256,1536]{2,1,0:T(8,128)S(1)} %get-tuple-element.26, f32[4,256]{1,0:T(4,128)S(1)} %get-tuple-element.29, f32[4,256]{1,0:T(4,128)S(1)} %get-tuple-element.30, f32[1536]{0:T(1024)S(1)} %copy-done.5, ...), kind=kLoop, calls=%fused_computation.20 | loop fusion | flops 17301504 | bytes 15751168 | tf_op jit(solution)/shard_map/convert_element_type | solution.py:36
  179.9 7.8 %copy.61 = bf16[160,96,256]{2,1,0:T(8,128)(2,1)} copy(bf16[160,96,256]{2,0,1:T(8,128)(2,1)S(1)} %convolution_convert_fusion.1) | data formatting | bytes 15728640
  187.7 15.3 %all-to-all-done.3 = bf16[2,16,96,256]{3,2,0,1:T(8,128)(2,1)} async-done(((bf16[2,16,96,256]{3,2,0,1:T(8,128)(2,1)}), bf16[2,16,96,256]{3,2,0,1:T(8,128)(2,1)}, u32[]{:S(2)}, u32[]{:S(2)}) %all-to-all-start.3) | async-done | bytes 1572896 | tf_op jit(solution)/shard_map/all_to_all | solution.py:81
  207.6 8.1 %copy.62 = bf16[160,96,256]{2,1,0:T(8,128)(2,1)} copy(bf16[160,96,256]{2,0,1:T(8,128)(2,1)S(1)} %convolution_convert_fusion) | data formatting | bytes 15728640
  (51 shorter events, 27.7 us)
Async XLA Ops:
  12.0 42.8 %all-to-all-start.1 = ((bf16[2,16,96,256]{3,2,0,1:T(8,128)(2,1)}), bf16[2,16,96,256]{3,2,0,1:T(8,128)(2,1)}, u32[]{:S(2)}, u32[]{:S(2)}) async-start(bf16[2,16,96,256]{3,2,0,1:T(8,128)(2,1)} %copy.51), calls=%async_computation.1 | async-start | bytes 3145728 | tf_op jit(solution)/shard_map/all_to_all | solution.py:63
  18.5 41.2 %copy-start.7 = (s32[64]{0:T(128)S(1)}, s32[64]{0:T(128)}, u32[]{:S(2)}) copy-start(s32[64]{0:T(128)} %param.18) | copy-start | bytes 772
  18.5 41.2 %copy-start = (s32[16,2]{0,1:T(2,128)S(1)}, s32[16,2]{0,1:T(2,128)}, u32[]{:S(2)}) copy-start(s32[16,2]{0,1:T(2,128)} %param.17) | copy-start | bytes 388
  18.5 42.3 %copy-start.6 = (s32[64]{0:T(128)S(1)}, s32[64]{0:T(128)}, u32[]{:S(2)}) copy-start(s32[64]{0:T(128)} %param.19) | copy-start | bytes 772
  18.5 43.3 %copy-start.1 = (bf16[4,256,1536]{2,1,0:T(8,128)(2,1)S(1)}, bf16[4,256,1536]{2,1,0:T(8,128)(2,1)}, u32[]{:S(2)}) copy-start(bf16[4,256,1536]{2,1,0:T(8,128)(2,1)} %param.12) | copy-start | bytes 9437188
  54.8 41.2 %all-to-all-start = ((bf16[2,16,96,256]{3,2,0,1:T(8,128)(2,1)}), bf16[2,16,96,256]{3,2,0,1:T(8,128)(2,1)}, u32[]{:S(2)}, u32[]{:S(2)}) async-start(bf16[2,16,96,256]{3,2,0,1:T(8,128)(2,1)} %copy.49), calls=%async_computation | async-start | bytes 3145728 | tf_op jit(solution)/shard_map/all_to_all | solution.py:64
  98.7 3.8 %copy-start.5 = (f32[1536]{0:T(1024)S(1)}, f32[1536]{0:T(1024)}, u32[]{:S(2)}) copy-start(f32[1536]{0:T(1024)} %param.14) | copy-start | bytes 18436
  102.5 4.4 %copy-start.2 = (bf16[4,1536,256]{2,1,0:T(8,128)(2,1)S(1)}, bf16[4,1536,256]{2,1,0:T(8,128)(2,1)}, u32[]{:S(2)}) copy-start(bf16[4,1536,256]{2,1,0:T(8,128)(2,1)} %gather_fusion.3) | copy-start | bytes 9437188
  102.5 4.4 %copy-start.3 = (bf16[4,256,1536]{2,1,0:T(8,128)(2,1)S(1)}, bf16[4,256,1536]{2,1,0:T(8,128)(2,1)}, u32[]{:S(2)}) copy-start(bf16[4,256,1536]{2,1,0:T(8,128)(2,1)} %param.13) | copy-start | bytes 9437188
  120.6 41.2 %all-to-all-start.2 = ((bf16[2,16,96,256]{3,2,0,1:T(8,128)(2,1)}), bf16[2,16,96,256]{3,2,0,1:T(8,128)(2,1)}, u32[]{:S(2)}, u32[]{:S(2)}) async-start(bf16[2,16,96,256]{3,2,0,1:T(8,128)(2,1)} %copy.55), calls=%async_computation.2 | async-start | bytes 3145728 | tf_op jit(solution)/shard_map/all_to_all | solution.py:81
  161.8 41.2 %all-to-all-start.3 = ((bf16[2,16,96,256]{3,2,0,1:T(8,128)(2,1)}), bf16[2,16,96,256]{3,2,0,1:T(8,128)(2,1)}, u32[]{:S(2)}, u32[]{:S(2)}) async-start(bf16[2,16,96,256]{3,2,0,1:T(8,128)(2,1)} %copy.59), calls=%async_computation.3 | async-start | bytes 3145728 | tf_op jit(solution)/shard_map/all_to_all | solution.py:81
  166.7 4.6 %copy-start.4 = (bf16[4,256,1536]{2,1,0:T(8,128)(2,1)S(1)}, bf16[4,256,1536]{2,1,0:T(8,128)(2,1)}, u32[]{:S(2)}) copy-start(bf16[4,256,1536]{2,1,0:T(8,128)(2,1)} %param.13) | copy-start | bytes 9437188
where the time goes:
time: 217 us; the launch traced here: 216 us
  waiting for transfers between devices  98.8 us (46%)
  local copies, waits for them, and re-layouts  62.5 us (29%)
  matrix products  25.1 us (12%)
  starting transfers between devices  21.3 us (10%)
  other arithmetic  7.25 us (3%)
    all_to_all x2, waiting for transfers between devices, exchange_back(): back = lax.all_to_all(scaled, 'dp', split_axis=1, concat_axis=1, tiled=True)  39.2 us
    all_to_all x1, waiting for transfers between devices, on_device(): lax.all_to_all(send_down, 'dp', split_axis=1, concat_axis=1, tiled=True)  33.4 us
    all_to_all x1, waiting for transfers between devices, on_device(): lax.all_to_all(send_up, 'dp', split_axis=1, concat_axis=1, tiled=True)  26.2 us
    unnamed x18, local copies, waits for them, and re-layouts  15.9 us
    all_to_all x2, starting transfers between devices, exchange_back(): back = lax.all_to_all(scaled, 'dp', split_axis=1, concat_axis=1, tiled=True)  9.83 us
    all_to_all x1, starting transfers between devices, on_device(): lax.all_to_all(send_down, 'dp', split_axis=1, concat_axis=1, tiled=True)  6.55 us
    reshape x2, local copies, waits for them, and re-layouts, exchange_back(): scaled = scaled.reshape(slots, devices, row_count, bottleneck)  5.37 us
    convert_element_type x2, local copies, waits for them, and re-layouts, exchange_back(): scaled = (grad * own_scale).astype(jnp.bfloat16)  5.15 us
  transfers between devices with their start and end apart: 4, of which 4 were waited for; matrix products, arithmetic and copies ran while one was open for 21% of the time, Pallas kernels for 0%

commit v1 on v0

--- a/solution.py
+++ b/solution.py
@@ -2,6 +2,28 @@
 import jax.numpy as jnp
 from jax import lax
 from jax.sharding import PartitionSpec as P
+
+
+def return_all_sample(vec, axis_no, buf):
+    local_out, block_next = (vec.shape[:axis_no], vec.shape[axis_no + 1 :])
+    return jnp.moveaxis(vec.reshape(*local_out, buf, -1, *block_next), axis_no, 0)
+
+
+def detail_the_figure(v0, array_axis):
+    v0 = jnp.moveaxis(v0, 0, array_axis)
+    w1 = v0.shape
+    return v0.reshape(*w1[:array_axis], w1[array_axis] * w1[array_axis + 1], *w1[array_axis + 2 :])
+
+
+def review_domain(mine, base_x, mesh_dim, load):
+    x_now, k_now = (lax.axis_size(mesh_dim), lax.axis_index(mesh_dim))
+    a_next = return_all_sample(mine, base_x, x_now)
+    block_list = [a_next[k_now]]
+    for q in range(1, x_now):
+        mid_arr = a_next[k_now ^ q]
+        block_list.append(lax.ppermute(mid_arr, mesh_dim, [(it, it ^ q) for it in range(x_now)]))
+    a_next = jnp.stack(block_list)[k_now ^ jnp.arange(x_now)]
+    return detail_the_figure(a_next, load)
 
 
 def local_pass(frames, cotangent, gain, w_down, w_up, live_mask, slot_select):
@@ -78,7 +100,7 @@
     def exchange_back(grad):
         scaled = (grad * own_scale).astype(jnp.bfloat16)
         scaled = scaled.reshape(slots, devices, row_count, bottleneck)
-        back = lax.all_to_all(scaled, "dp", split_axis=1, concat_axis=1, tiled=True)
+        back = review_domain(scaled, 1, "dp", 1)
         return back.reshape(slots * devices, row_count, bottleneck)
 
     back_down = exchange_back(grad_down)

time: 217 us -> 315 us (1.45)
  starting transfers between devices: 21.3 us -> 66.4 us
  local copies, waits for them, and re-layouts: 62.5 us -> 85.8 us
  waiting for transfers between devices: 98.8 us -> 122 us
    ppermute x0 -> x30, waiting for transfers between devices: none -> 60.3 us  [review_domain(): lax.ppermute(mid_arr, mesh_dim, [(it, it ^ q) for it in range(x_now)])]
    ppermute x0 -> x30, starting transfers between devices: none -> 54.9 us  [review_domain(): lax.ppermute(mid_arr, mesh_dim, [(it, it ^ q) for it in range(x_now)])]
    all_to_all x2 -> x0, waiting for transfers between devices: 39.2 us -> none  [exchange_back(): back = lax.all_to_all(scaled, 'dp', split_axis=1, concat_axis=1, tiled=True)]
    unnamed x18 -> x50, local copies, waits for them, and re-layouts: 15.9 us -> 36.3 us
    all_to_all x2 -> x0, starting transfers between devices: 9.83 us -> none  [exchange_back(): back = lax.all_to_all(scaled, 'dp', split_axis=1, concat_axis=1, tiled=True)]
    gather x0 -> x2, local copies, waits for them, and re-layouts: none -> 6.39 us  [review_domain(): a_next = jnp.stack(block_list)[k_now ^ jnp.arange(x_now)]]
    reshape x2 -> x0, local copies, waits for them, and re-layouts: 5.37 us -> none  [exchange_back(): scaled = scaled.reshape(slots, devices, row_count, bottleneck)]
    all_to_all x2 -> x0, local copies, waits for them, and re-layouts: 4.57 us -> none  [exchange_back(): back = lax.all_to_all(scaled, 'dp', split_axis=1, concat_axis=1, tiled=True)]
  transfers between devices with their start and end apart: 4 -> 32, of which waited for: 4 -> 23; matrix products, arithmetic and copies ran while one was open for 21% -> 13% of each run, Pallas kernels for 0% -> 0%
where the time goes in v1:
time: 315 us; the launch traced here: 311 us
  waiting for transfers between devices  122 us (39%)
  local copies, waits for them, and re-layouts  85.8 us (27%)
  starting transfers between devices  66.4 us (21%)
  matrix products  27.2 us (9%)
  other arithmetic  9.43 us (3%)
    ppermute x30, waiting for transfers between devices, review_domain(): lax.ppermute(mid_arr, mesh_dim, [(it, it ^ q) for it in range(x_now)])  60.3 us
    ppermute x30, starting transfers between devices, review_domain(): lax.ppermute(mid_arr, mesh_dim, [(it, it ^ q) for it in range(x_now)])  54.9 us
    unnamed x50, local copies, waits for them, and re-layouts  36.3 us
    all_to_all x1, waiting for transfers between devices, on_device(): lax.all_to_all(send_down, 'dp', split_axis=1, concat_axis=1, tiled=True)  35 us
    all_to_all x1, waiting for transfers between devices, on_device(): lax.all_to_all(send_up, 'dp', split_axis=1, concat_axis=1, tiled=True)  26.3 us
    dot_general x1, matrix products, local_pass(): jnp.einsum('ufr,udr->ufd', d_pre, w_down, preferred_element_type=jnp.floa...  6.84 us
    all_to_all x1, starting transfers between devices, on_device(): lax.all_to_all(send_down, 'dp', split_axis=1, concat_axis=1, tiled=True)  6.55 us
    gather x2, local copies, waits for them, and re-layouts, review_domain(): a_next = jnp.stack(block_list)[k_now ^ jnp.arange(x_now)]  6.39 us
  transfers between devices with their start and end apart: 32, of which 23 were waited for; matrix products, arithmetic and copies ran while one was open for 13% of the time, Pallas kernels for 0%

profile of v1, /device:TPU:13, one launch (start us, length us, event | category | flops | bytes accessed | tf_op | source)
XLA Modules:
  0.0 311.3 jit_solution(7232778948457226698)
XLA Ops:
  2.3 3.9 %gather_fusion.6 = bf16[32,96,256]{2,1,0:T(8,128)(2,1)S(1)} fusion(bf16[160,96,256]{2,1,0:T(8,128)(2,1)} %param.15, s32[1024]{0:T(1024)S(1)} %get-tuple-element.63), kind=kCustom, calls=%fused_computation.2.clone | custom fusion | bytes 3145856 | tf_op jit(solution)/shard_map/jit(_take)/gather | solution.py:79
  6.2 5.0 %gather_fusion.4 = bf16[32,96,256]{2,1,0:T(8,128)(2,1)} fusion(bf16[160,96,256]{2,1,0:T(8,128)(2,1)} %param.16, s32[1024]{0:T(1024)S(1)} %get-tuple-element.63), kind=kCustom, calls=%fused_computation.clone | custom fusion | bytes 3145856 | tf_op jit(solution)/shard_map/jit(_take)/gather | solution.py:82
  14.2 6.6 %all-to-all-start.1 = ((bf16[2,16,96,256]{3,2,0,1:T(8,128)(2,1)}), bf16[2,16,96,256]{3,2,0,1:T(8,128)(2,1)}, u32[]{:S(2)}, u32[]{:S(2)}) async-start(bf16[2,16,96,256]{3,2,0,1:T(8,128)(2,1)} %copy.65), calls=%async_computation.1 | async-start | bytes 3145728 | tf_op jit(solution)/shard_map/all_to_all | solution.py:85
  22.1 35.0 %all-to-all-done.1 = bf16[2,16,96,256]{3,2,0,1:T(8,128)(2,1)} async-done(((bf16[2,16,96,256]{3,2,0,1:T(8,128)(2,1)}), bf16[2,16,96,256]{3,2,0,1:T(8,128)(2,1)}, u32[]{:S(2)}, u32[]{:S(2)}) %all-to-all-start.1) | async-done | bytes 1572896 | tf_op jit(solution)/shard_map/all_to_all | solution.py:85
  57.1 4.9 %all-to-all-start = ((bf16[2,16,96,256]{3,2,0,1:T(8,128)(2,1)}), bf16[2,16,96,256]{3,2,0,1:T(8,128)(2,1)}, u32[]{:S(2)}, u32[]{:S(2)}) async-start(bf16[2,16,96,256]{3,2,0,1:T(8,128)(2,1)} %copy.63), calls=%async_computation | async-start | bytes 3145728 | tf_op jit(solution)/shard_map/all_to_all | solution.py:86
  68.2 3.8 %gather_fusion.7 = bf16[4,1536,256]{2,1,0:T(8,128)(2,1)} fusion(bf16[2,1536,256]{2,1,0:T(8,128)(2,1)} %bitcast.200, s32[1024]{0:T(1024)S(1)} %pad_clamp_fusion.2), kind=kCustom, calls=%fused_computation.3.clone | custom fusion | bytes 6291472 | tf_op jit(solution)/shard_map/jit(_take)/gather | solution.py:89
  72.0 26.3 %all-to-all-done = bf16[2,16,96,256]{3,2,0,1:T(8,128)(2,1)} async-done(((bf16[2,16,96,256]{3,2,0,1:T(8,128)(2,1)}), bf16[2,16,96,256]{3,2,0,1:T(8,128)(2,1)}, u32[]{:S(2)}, u32[]{:S(2)}) %all-to-all-start) | async-done | bytes 1572896 | tf_op jit(solution)/shard_map/all_to_all | solution.py:86
  100.9 3.8 %gather_fusion.5 = bf16[4,1536,256]{2,1,0:T(8,128)(2,1)} fusion(bf16[2,1536,256]{2,1,0:T(8,128)(2,1)} %bitcast.199, s32[1024]{0:T(1024)S(1)} %pad_clamp_fusion.2), kind=kCustom, calls=%fused_computation.1.clone | custom fusion | bytes 6291472 | tf_op jit(solution)/shard_map/jit(_take)/gather | solution.py:90
  104.8 4.4 %multiply_convert_fusion = (bf16[4,256,256]{2,1,0:T(8,128)(2,1)}, f32[4,256,256]{2,1,0:T(8,128)S(1)}) fusion(bf16[4,1536,256]{2,1,0:T(8,128)(2,1)} %gather_fusion.7, pred[4]{0:T(512)(128)(4,1)S(1)} %get-tuple-element.25, bf16[4,256,1536]{2,1,0:T(8,128)(2,1)S(1)} %copy-done.1, f32[1536]{0:T(1024)S(1)} %copy-done.6, f32[4,256]{1,0:T(4,128)S(1)} %add_rsqrt_fusion, ...), kind=kOutput, calls=%fused_computation.53 | convolution fusion | flops 816054272 | bytes 7878660 | tf_op jit(solution)/shard_map/ufd,udr->ufr/dot_general | solution.py:37
  113.4 6.8 %multiply_reduce_fusion = (f32[4,256]{1,0:T(4,128)S(1)}, f32[4,256]{1,0:T(4,128)S(1)}, f32[4,256,1536]{2,1,0:T(8,128)}) fusion(f32[1536]{0:T(1024)S(1)} %copy-done.6, f32[4,256]{1,0:T(4,128)S(1)} %add_rsqrt_fusion, f32[4,256]{1,0:T(4,128)S(1)} %broadcast_multiply_fusion.2, bf16[4,256,1536]{2,1,0:T(8,128)(2,1)S(1)} %copy-done.1, ...), kind=kOutput, calls=%fused_computation.24 | convolution fusion | flops 817887232 | bytes 13129732 | tf_op jit(solution)/shard_map/ufr,udr->ufd/dot_general | solution.py:51
  122.3 5.1 %fusion.25 = bf16[2,1536,256]{1,2,0:T(8,128)(2,1)} fusion(bf16[4,256,1536]{2,1,0:T(8,128)(2,1)} %param.13, pred[4,256]{1,0:T(4,128)(4,1)S(1)} %iota_compare_fusion.2, f32[2]{0:T(128)S(1)} %and_select_fusion.1, bf16[4,256,256]{1,2,0:T(8,128)(2,1)} %copy.72, bf16[2,4]{1,0:T(2,128)(2,1)S(1)} %compare_convert_fusion), kind=kOutput, calls=%fused_computation.38 | convolution fusion | flops 1614282752 | bytes 5243928 | tf_op jit(solution)/shard_map/ufd,sufr->sdr/dot_general | solution.py:42
  129.9 4.1 %fusion.28 = bf16[2,1536,256]{1,2,0:T(8,128)(2,1)} fusion(bf16[4,256,1536]{2,1,0:T(8,128)(2,1)S(1)} %copy-done.1, f32[1536]{0:T(1024)S(1)} %copy-done.6, f32[4,256]{1,0:T(4,128)S(1)} %add_rsqrt_fusion, f32[4,256]{1,0:T(4,128)S(1)} %broadcast_multiply_fusion.2, f32[2]{0:T(128)S(1)} %and_select_fusion.1, bf16[2,4]{1,0:T(2,128)(2,1)S(1)} %compare_convert_fusion, ...), kind=kOutput, calls=%fused_computation.39 | convolution fusion | flops 1620574208 | bytes 5257240 | tf_op jit(solution)/shard_map/ufd,sufr->sdr/dot_general | solution.py:48
  144.9 5.9 %fusion.10 = bf16[4,256,1536]{2,1,0:T(8,128)(2,1)} fusion(bf16[4,256,1536]{2,1,0:T(8,128)(2,1)S(1)} %copy-done.1, bf16[4,256,1536]{2,1,0:T(8,128)(2,1)S(1)} %copy-done.5, f32[4,256,1536]{2,1,0:T(8,128)} %get-tuple-element.59, f32[4,256]{1,0:T(4,128)S(1)} %broadcast_multiply_fusion, f32[4,256]{1,0:T(4,128)S(1)} %broadcast_multiply_fusion.1, ...), kind=kLoop, calls=%fused_computation.22 | loop fusion | flops 17301504 | bytes 15751168 | tf_op jit(solution)/shard_map/convert_element_type | solution.py:58
  152.1 4.0 %collective-permute-done.1 = bf16[2,1,96,256]{3,2,0,1:T(8,128)(2,1)S(1)} collective-permute-done((bf16[2,1,96,256]{3,2,0,1:T(8,128)(2,1)S(1)}, bf16[2,1,96,256]{3,2,0,1:T(8,128)(2,1)S(1)}, u32[]{:S(2)}, u32[]{:S(2)}) %collective-permute-start.1) | collective-permute-done | bytes 98336 | tf_op jit(solution)/shard_map/ppermute | solution.py:24
  187.1 5.4 %collective-permute-start.8 = (bf16[2,1,96,256]{3,2,0,1:T(8,128)(2,1)S(1)}, bf16[2,1,96,256]{3,2,0,1:T(8,128)(2,1)S(1)}, u32[]{:S(2)}, u32[]{:S(2)}) collective-permute-start(bf16[2,1,96,256]{3,2,0,1:T(8,128)(2,1)S(1)} %get-tuple-element.48), channel_id=1, source_target_pairs={{0,9},{1,8},{2,11},{3,10},{4,13},{5,12},{6,15},{7,14},{8,1},{9,0},... | collective-permute-start | bytes 294920 | tf_op jit(solution)/shard_map/ppermute | solution.py:24
  195.8 5.5 %collective-permute-done.9 = bf16[2,1,96,256]{3,2,0,1:T(8,128)(2,1)S(1)} collective-permute-done((bf16[2,1,96,256]{3,2,0,1:T(8,128)(2,1)S(1)}, bf16[2,1,96,256]{3,2,0,1:T(8,128)(2,1)S(1)}, u32[]{:S(2)}, u32[]{:S(2)}) %collective-permute-start.9) | collective-permute-done | bytes 98336 | tf_op jit(solution)/shard_map/ppermute | solution.py:24
  201.3 4.7 %collective-permute-start.10 = (bf16[2,1,96,256]{3,2,0,1:T(8,128)(2,1)S(1)}, bf16[2,1,96,256]{3,2,0,1:T(8,128)(2,1)S(1)}, u32[]{:S(2)}, u32[]{:S(2)}) collective-permute-start(bf16[2,1,96,256]{3,2,0,1:T(8,128)(2,1)S(1)} %get-tuple-element.46), channel_id=1, source_target_pairs={{0,11},{1,10},{2,9},{3,8},{4,15},{5,14},{6,13},{7,12},{8,3},{9,2},... | collective-permute-start | bytes 294920 | tf_op jit(solution)/shard_map/ppermute | solution.py:24
  227.1 5.7 %collective-permute-start.18 = (bf16[2,1,96,256]{3,2,0,1:T(8,128)(2,1)S(1)}, bf16[2,1,96,256]{3,2,0,1:T(8,128)(2,1)S(1)}, u32[]{:S(2)}, u32[]{:S(2)}) collective-permute-start(bf16[2,1,96,256]{3,2,0,1:T(8,128)(2,1)S(1)} %get-tuple-element.38), channel_id=1, source_target_pairs={{0,4},{1,5},{2,6},{3,7},{4,0},{5,1},{6,2},{7,3},{8,12},{9,13},{10,... | collective-permute-start | bytes 294920 | tf_op jit(solution)/shard_map/ppermute | solution.py:24
  241.7 4.4 %collective-permute-done.20 = bf16[2,1,96,256]{3,2,0,1:T(8,128)(2,1)S(1)} collective-permute-done((bf16[2,1,96,256]{3,2,0,1:T(8,128)(2,1)S(1)}, bf16[2,1,96,256]{3,2,0,1:T(8,128)(2,1)S(1)}, u32[]{:S(2)}, u32[]{:S(2)}) %collective-permute-start.20) | collective-permute-done | bytes 98336 | tf_op jit(solution)/shard_map/ppermute | solution.py:24
  256.6 4.1 %collective-permute-start.23 = (bf16[2,1,96,256]{3,2,0,1:T(8,128)(2,1)S(1)}, bf16[2,1,96,256]{3,2,0,1:T(8,128)(2,1)S(1)}, u32[]{:S(2)}, u32[]{:S(2)}) collective-permute-start(bf16[2,1,96,256]{3,2,0,1:T(8,128)(2,1)S(1)} %get-tuple-element.33), channel_id=1, source_target_pairs={{0,9},{1,8},{2,11},{3,10},{4,13},{5,12},{6,15},{7,14},{8,1},{9,0},... | collective-permute-start | bytes 294920 | tf_op jit(solution)/shard_map/ppermute | solution.py:24
  263.7 4.2 %collective-permute-start.24 = (bf16[2,1,96,256]{3,2,0,1:T(8,128)(2,1)S(1)}, bf16[2,1,96,256]{3,2,0,1:T(8,128)(2,1)S(1)}, u32[]{:S(2)}, u32[]{:S(2)}) collective-permute-start(bf16[2,1,96,256]{3,2,0,1:T(8,128)(2,1)S(1)} %get-tuple-element.32), channel_id=1, source_target_pairs={{0,10},{1,11},{2,8},{3,9},{4,14},{5,15},{6,12},{7,13},{8,2},{9,3},... | collective-permute-start | bytes 294920 | tf_op jit(solution)/shard_map/ppermute | solution.py:24
  270.7 4.1 %collective-permute-start.25 = (bf16[2,1,96,256]{3,2,0,1:T(8,128)(2,1)S(1)}, bf16[2,1,96,256]{3,2,0,1:T(8,128)(2,1)S(1)}, u32[]{:S(2)}, u32[]{:S(2)}) collective-permute-start(bf16[2,1,96,256]{3,2,0,1:T(8,128)(2,1)S(1)} %get-tuple-element.31), channel_id=1, source_target_pairs={{0,11},{1,10},{2,9},{3,8},{4,15},{5,14},{6,13},{7,12},{8,3},{9,2},... | collective-permute-start | bytes 294920 | tf_op jit(solution)/shard_map/ppermute | solution.py:24
  293.1 7.8 %copy.78 = bf16[160,96,256]{2,1,0:T(8,128)(2,1)} copy(bf16[160,96,256]{2,0,1:T(8,128)(2,1)S(1)} %convolution_convert_fusion) | data formatting | bytes 15728640
  303.3 8.1 %copy.77 = bf16[160,96,256]{2,1,0:T(8,128)(2,1)} copy(bf16[160,96,256]{2,0,1:T(8,128)(2,1)S(1)} %convolution_convert_fusion.1) | data formatting | bytes 15728640
  (145 shorter events, 136.7 us)
Async XLA Ops:
  14.2 42.8 %all-to-all-start.1 = ((bf16[2,16,96,256]{3,2,0,1:T(8,128)(2,1)}), bf16[2,16,96,256]{3,2,0,1:T(8,128)(2,1)}, u32[]{:S(2)}, u32[]{:S(2)}) async-start(bf16[2,16,96,256]{3,2,0,1:T(8,128)(2,1)} %copy.65), calls=%async_computation.1 | async-start | bytes 3145728 | tf_op jit(solution)/shard_map/all_to_all | solution.py:85
  57.1 41.2 %all-to-all-start = ((bf16[2,16,96,256]{3,2,0,1:T(8,128)(2,1)}), bf16[2,16,96,256]{3,2,0,1:T(8,128)(2,1)}, u32[]{:S(2)}, u32[]{:S(2)}) async-start(bf16[2,16,96,256]{3,2,0,1:T(8,128)(2,1)} %copy.63), calls=%async_computation | async-start | bytes 3145728 | tf_op jit(solution)/shard_map/all_to_all | solution.py:86
  140.0 75.8 %collective-permute-start.14 = (bf16[2,1,96,256]{3,2,0,1:T(8,128)(2,1)S(1)}, bf16[2,1,96,256]{3,2,0,1:T(8,128)(2,1)S(1)}, u32[]{:S(2)}, u32[]{:S(2)}) collective-permute-start(bf16[2,1,96,256]{3,2,0,1:T(8,128)(2,1)S(1)} %get-tuple-element.42), channel_id=1, source_target_pairs={{0,15},{1,14},{2,13},{3,12},{4,11},{5,10},{6,9},{7,8},{8,7},{9,6},... | collective-permute-start | bytes 294920 | tf_op jit(solution)/shard_map/ppermute | solution.py:24
  141.7 73.0 %collective-permute-start.13 = (bf16[2,1,96,256]{3,2,0,1:T(8,128)(2,1)S(1)}, bf16[2,1,96,256]{3,2,0,1:T(8,128)(2,1)S(1)}, u32[]{:S(2)}, u32[]{:S(2)}) collective-permute-start(bf16[2,1,96,256]{3,2,0,1:T(8,128)(2,1)S(1)} %get-tuple-element.43), channel_id=1, source_target_pairs={{0,14},{1,15},{2,12},{3,13},{4,10},{5,11},{6,8},{7,9},{8,6},{9,7},... | collective-permute-start | bytes 294920 | tf_op jit(solution)/shard_map/ppermute | solution.py:24
  142.5 69.7 %collective-permute-start.12 = (bf16[2,1,96,256]{3,2,0,1:T(8,128)(2,1)S(1)}, bf16[2,1,96,256]{3,2,0,1:T(8,128)(2,1)S(1)}, u32[]{:S(2)}, u32[]{:S(2)}) collective-permute-start(bf16[2,1,96,256]{3,2,0,1:T(8,128)(2,1)S(1)} %get-tuple-element.44), channel_id=1, source_target_pairs={{0,13},{1,12},{2,15},{3,14},{4,9},{5,8},{6,11},{7,10},{8,5},{9,4},... | collective-permute-start | bytes 294920 | tf_op jit(solution)/shard_map/ppermute | solution.py:24
  142.5 69.0 %collective-permute-start.11 = (bf16[2,1,96,256]{3,2,0,1:T(8,128)(2,1)S(1)}, bf16[2,1,96,256]{3,2,0,1:T(8,128)(2,1)S(1)}, u32[]{:S(2)}, u32[]{:S(2)}) collective-permute-start(bf16[2,1,96,256]{3,2,0,1:T(8,128)(2,1)S(1)} %get-tuple-element.45), channel_id=1, source_target_pairs={{0,12},{1,13},{2,14},{3,15},{4,8},{5,9},{6,10},{7,11},{8,4},{9,5},... | collective-permute-start | bytes 294920 | tf_op jit(solution)/shard_map/ppermute | solution.py:24
  144.5 6.9 %collective-permute-start = (bf16[2,1,96,256]{3,2,0,1:T(8,128)(2,1)S(1)}, bf16[2,1,96,256]{3,2,0,1:T(8,128)(2,1)S(1)}, u32[]{:S(2)}, u32[]{:S(2)}) collective-permute-start(bf16[2,1,96,256]{3,2,0,1:T(8,128)(2,1)S(1)} %get-tuple-element.56), channel_id=1, source_target_pairs={{0,1},{1,0},{2,3},{3,2},{4,5},{5,4},{6,7},{7,6},{8,9},{9,8},{10,11... | collective-permute-start | bytes 294920 | tf_op jit(solution)/shard_map/ppermute | solution.py:24
  156.1 5.3 %collective-permute-start.2 = (bf16[2,1,96,256]{3,2,0,1:T(8,128)(2,1)S(1)}, bf16[2,1,96,256]{3,2,0,1:T(8,128)(2,1)S(1)}, u32[]{:S(2)}, u32[]{:S(2)}) collective-permute-start(bf16[2,1,96,256]{3,2,0,1:T(8,128)(2,1)S(1)} %get-tuple-element.54), channel_id=1, source_target_pairs={{0,3},{1,2},{2,1},{3,0},{4,7},{5,6},{6,5},{7,4},{8,11},{9,10},{10,... | collective-permute-start | bytes 294920 | tf_op jit(solution)/shard_map/ppermute | solution.py:24
  166.5 5.5 %collective-permute-start.4 = (bf16[2,1,96,256]{3,2,0,1:T(8,128)(2,1)S(1)}, bf16[2,1,96,256]{3,2,0,1:T(8,128)(2,1)S(1)}, u32[]{:S(2)}, u32[]{:S(2)}) collective-permute-start(bf16[2,1,96,256]{3,2,0,1:T(8,128)(2,1)S(1)} %get-tuple-element.52), channel_id=1, source_target_pairs={{0,5},{1,4},{2,7},{3,6},{4,1},{5,0},{6,3},{7,2},{8,13},{9,12},{10,... | collective-permute-start | bytes 294920 | tf_op jit(solution)/shard_map/ppermute | solution.py:24
  176.9 5.8 %collective-permute-start.6 = (bf16[2,1,96,256]{3,2,0,1:T(8,128)(2,1)S(1)}, bf16[2,1,96,256]{3,2,0,1:T(8,128)(2,1)S(1)}, u32[]{:S(2)}, u32[]{:S(2)}) collective-permute-start(bf16[2,1,96,256]{3,2,0,1:T(8,128)(2,1)S(1)} %get-tuple-element.50), channel_id=1, source_target_pairs={{0,7},{1,6},{2,5},{3,4},{4,3},{5,2},{6,1},{7,0},{8,15},{9,14},{10,... | collective-permute-start | bytes 294920 | tf_op jit(solution)/shard_map/ppermute | solution.py:24
  187.1 8.0 %collective-permute-start.8 = (bf16[2,1,96,256]{3,2,0,1:T(8,128)(2,1)S(1)}, bf16[2,1,96,256]{3,2,0,1:T(8,128)(2,1)S(1)}, u32[]{:S(2)}, u32[]{:S(2)}) collective-permute-start(bf16[2,1,96,256]{3,2,0,1:T(8,128)(2,1)S(1)} %get-tuple-element.48), channel_id=1, source_target_pairs={{0,9},{1,8},{2,11},{3,10},{4,13},{5,12},{6,15},{7,14},{8,1},{9,0},... | collective-permute-start | bytes 294920 | tf_op jit(solution)/shard_map/ppermute | solution.py:24
  195.2 6.1 %collective-permute-start.9 = (bf16[2,1,96,256]{3,2,0,1:T(8,128)(2,1)S(1)}, bf16[2,1,96,256]{3,2,0,1:T(8,128)(2,1)S(1)}, u32[]{:S(2)}, u32[]{:S(2)}) collective-permute-start(bf16[2,1,96,256]{3,2,0,1:T(8,128)(2,1)S(1)} %get-tuple-element.47), channel_id=1, source_target_pairs={{0,10},{1,11},{2,8},{3,9},{4,14},{5,15},{6,12},{7,13},{8,2},{9,3},... | collective-permute-start | bytes 294920 | tf_op jit(solution)/shard_map/ppermute | solution.py:24
  201.3 7.5 %collective-permute-start.10 = (bf16[2,1,96,256]{3,2,0,1:T(8,128)(2,1)S(1)}, bf16[2,1,96,256]{3,2,0,1:T(8,128)(2,1)S(1)}, u32[]{:S(2)}, u32[]{:S(2)}) collective-permute-start(bf16[2,1,96,256]{3,2,0,1:T(8,128)(2,1)S(1)} %get-tuple-element.46), channel_id=1, source_target_pairs={{0,11},{1,10},{2,9},{3,8},{4,15},{5,14},{6,13},{7,12},{8,3},{9,2},... | collective-permute-start | bytes 294920 | tf_op jit(solution)/shard_map/ppermute | solution.py:24
  208.8 76.7 %collective-permute-start.29 = (bf16[2,1,96,256]{3,2,0,1:T(8,128)(2,1)S(1)}, bf16[2,1,96,256]{3,2,0,1:T(8,128)(2,1)S(1)}, u32[]{:S(2)}, u32[]{:S(2)}) collective-permute-start(bf16[2,1,96,256]{3,2,0,1:T(8,128)(2,1)S(1)} %get-tuple-element.27), channel_id=1, source_target_pairs={{0,15},{1,14},{2,13},{3,12},{4,11},{5,10},{6,9},{7,8},{8,7},{9,6},... | collective-permute-start | bytes 294920 | tf_op jit(solution)/shard_map/ppermute | solution.py:24
  211.6 68.5 %collective-permute-start.28 = (bf16[2,1,96,256]{3,2,0,1:T(8,128)(2,1)S(1)}, bf16[2,1,96,256]{3,2,0,1:T(8,128)(2,1)S(1)}, u32[]{:S(2)}, u32[]{:S(2)}) collective-permute-start(bf16[2,1,96,256]{3,2,0,1:T(8,128)(2,1)S(1)} %get-tuple-element.28), channel_id=1, source_target_pairs={{0,14},{1,15},{2,12},{3,13},{4,10},{5,11},{6,8},{7,9},{8,6},{9,7},... | collective-permute-start | bytes 294920 | tf_op jit(solution)/shard_map/ppermute | solution.py:24
  212.2 67.2 %collective-permute-start.27 = (bf16[2,1,96,256]{3,2,0,1:T(8,128)(2,1)S(1)}, bf16[2,1,96,256]{3,2,0,1:T(8,128)(2,1)S(1)}, u32[]{:S(2)}, u32[]{:S(2)}) collective-permute-start(bf16[2,1,96,256]{3,2,0,1:T(8,128)(2,1)S(1)} %get-tuple-element.29), channel_id=1, source_target_pairs={{0,13},{1,12},{2,15},{3,14},{4,9},{5,8},{6,11},{7,10},{8,5},{9,4},... | collective-permute-start | bytes 294920 | tf_op jit(solution)/shard_map/ppermute | solution.py:24
  214.7 64.0 %collective-permute-start.26 = (bf16[2,1,96,256]{3,2,0,1:T(8,128)(2,1)S(1)}, bf16[2,1,96,256]{3,2,0,1:T(8,128)(2,1)S(1)}, u32[]{:S(2)}, u32[]{:S(2)}) collective-permute-start(bf16[2,1,96,256]{3,2,0,1:T(8,128)(2,1)S(1)} %get-tuple-element.30), channel_id=1, source_target_pairs={{0,12},{1,13},{2,14},{3,15},{4,8},{5,9},{6,10},{7,11},{8,4},{9,5},... | collective-permute-start | bytes 294920 | tf_op jit(solution)/shard_map/ppermute | solution.py:24
  221.9 5.3 %collective-permute-start.17 = (bf16[2,1,96,256]{3,2,0,1:T(8,128)(2,1)S(1)}, bf16[2,1,96,256]{3,2,0,1:T(8,128)(2,1)S(1)}, u32[]{:S(2)}, u32[]{:S(2)}) collective-permute-start(bf16[2,1,96,256]{3,2,0,1:T(8,128)(2,1)S(1)} %get-tuple-element.39), channel_id=1, source_target_pairs={{0,3},{1,2},{2,1},{3,0},{4,7},{5,6},{6,5},{7,4},{8,11},{9,10},{10,... | collective-permute-start | bytes 294920 | tf_op jit(solution)/shard_map/ppermute | solution.py:24
  227.1 8.1 %collective-permute-start.18 = (bf16[2,1,96,256]{3,2,0,1:T(8,128)(2,1)S(1)}, bf16[2,1,96,256]{3,2,0,1:T(8,128)(2,1)S(1)}, u32[]{:S(2)}, u32[]{:S(2)}) collective-permute-start(bf16[2,1,96,256]{3,2,0,1:T(8,128)(2,1)S(1)} %get-tuple-element.38), channel_id=1, source_target_pairs={{0,4},{1,5},{2,6},{3,7},{4,0},{5,1},{6,2},{7,3},{8,12},{9,13},{10,... | collective-permute-start | bytes 294920 | tf_op jit(solution)/shard_map/ppermute | solution.py:24
  235.2 5.8 %collective-permute-start.19 = (bf16[2,1,96,256]{3,2,0,1:T(8,128)(2,1)S(1)}, bf16[2,1,96,256]{3,2,0,1:T(8,128)(2,1)S(1)}, u32[]{:S(2)}, u32[]{:S(2)}) collective-permute-start(bf16[2,1,96,256]{3,2,0,1:T(8,128)(2,1)S(1)} %get-tuple-element.37), channel_id=1, source_target_pairs={{0,5},{1,4},{2,7},{3,6},{4,1},{5,0},{6,3},{7,2},{8,13},{9,12},{10,... | collective-permute-start | bytes 294920 | tf_op jit(solution)/shard_map/ppermute | solution.py:24
  246.1 6.0 %collective-permute-start.21 = (bf16[2,1,96,256]{3,2,0,1:T(8,128)(2,1)S(1)}, bf16[2,1,96,256]{3,2,0,1:T(8,128)(2,1)S(1)}, u32[]{:S(2)}, u32[]{:S(2)}) collective-permute-start(bf16[2,1,96,256]{3,2,0,1:T(8,128)(2,1)S(1)} %get-tuple-element.35), channel_id=1, source_target_pairs={{0,7},{1,6},{2,5},{3,4},{4,3},{5,2},{6,1},{7,0},{8,15},{9,14},{10,... | collective-permute-start | bytes 294920 | tf_op jit(solution)/shard_map/ppermute | solution.py:24
  256.6 7.2 %collective-permute-start.23 = (bf16[2,1,96,256]{3,2,0,1:T(8,128)(2,1)S(1)}, bf16[2,1,96,256]{3,2,0,1:T(8,128)(2,1)S(1)}, u32[]{:S(2)}, u32[]{:S(2)}) collective-permute-start(bf16[2,1,96,256]{3,2,0,1:T(8,128)(2,1)S(1)} %get-tuple-element.33), channel_id=1, source_target_pairs={{0,9},{1,8},{2,11},{3,10},{4,13},{5,12},{6,15},{7,14},{8,1},{9,0},... | collective-permute-start | bytes 294920 | tf_op jit(solution)/shard_map/ppermute | solution.py:24
  263.7 7.0 %collective-permute-start.24 = (bf16[2,1,96,256]{3,2,0,1:T(8,128)(2,1)S(1)}, bf16[2,1,96,256]{3,2,0,1:T(8,128)(2,1)S(1)}, u32[]{:S(2)}, u32[]{:S(2)}) collective-permute-start(bf16[2,1,96,256]{3,2,0,1:T(8,128)(2,1)S(1)} %get-tuple-element.32), channel_id=1, source_target_pairs={{0,10},{1,11},{2,8},{3,9},{4,14},{5,15},{6,12},{7,13},{8,2},{9,3},... | collective-permute-start | bytes 294920 | tf_op jit(solution)/shard_map/ppermute | solution.py:24
  270.7 7.4 %collective-permute-start.25 = (bf16[2,1,96,256]{3,2,0,1:T(8,128)(2,1)S(1)}, bf16[2,1,96,256]{3,2,0,1:T(8,128)(2,1)S(1)}, u32[]{:S(2)}, u32[]{:S(2)}) collective-permute-start(bf16[2,1,96,256]{3,2,0,1:T(8,128)(2,1)S(1)} %get-tuple-element.31), channel_id=1, source_target_pairs={{0,11},{1,10},{2,9},{3,8},{4,15},{5,14},{6,13},{7,12},{8,3},{9,2},... | collective-permute-start | bytes 294920 | tf_op jit(solution)/shard_map/ppermute | solution.py:24
  (17 other events, 226.0 us)
